TPU v7x, 512 devices: a whole 4x4x16 slice. The times are simulated.
512 devices in a mesh: pool: 128 (over x, z, core), tp: 4 (over y).
Axes of the slice: x: 4, y: 4, z: 16, core: 2. Of those that a mesh axis runs over, the one named last changes fastest.
Arguments:
- hidden_rows: bfloat16 [16384, 8192], P('pool', 'tp'), may hold values from -6 to 6
- kv_weight: bfloat16 [8192, 1024], P('tp', 'pool'), may hold values from -0.0625 to 0.0625
- queries: bfloat16 [16384, 4096], P('pool', 'tp'), may hold values from -5 to 5
- cache_table: bfloat16 [1024, 128, 1024], P('pool', None, 'tp'), may hold values from -5 to 5
- retrieval: int32 [128, 64], P('pool'), may hold values from 0 to 1023, as said below
- pattern: int32 [128, 2, 64], P('pool'), may hold values 0 or 1
Outputs:
- attended: bfloat16 [16384, 4096], P('pool', 'tp')
- fresh_kv: bfloat16 [16384, 1024], P('pool', 'tp')
Inputs may be any that keep to these rules, and one draw needn't show every extreme that they name: `retrieval`: each request names 64 blocks held by 64 different devices (block b is held by device b // 8); one device, drawn from the seed, holds a block named by every request.
All inputs are finite; a program needn't handle non-finite values. No bound on the sum of `pattern` on one device may be relied on, other than what follows from the above.
Results may differ from a plain program's by a relative error of at most 0.025.
Values may be sent and summed in bfloat16 or wider, within the bound.
No kernel may reach another device: no remote copies, remote signals or barrier semaphores. Data moves between devices by JAX's collectives and lax.ppermute only.
A program may use at most 192 MiB of HBM per device.

v0:
```python
import math
import jax
import jax.numpy as jnp
from jax import lax
from jax.sharding import PartitionSpec as P

HD = 128
QH = 32
KVH = 4
BLK = 128
RBLK = 64


def rows_by_keys(left, right):
    return lax.dot_general(
        left, right, (((1,), (1,)), ((), ())), preferred_element_type=jnp.float32
    )


def body(hidden_rows, kv_weight, queries, cache_table, retrieval, pattern):
    partial_kv = jnp.dot(
        hidden_rows,
        lax.all_gather(kv_weight, "pool", axis=1, tiled=True),
        preferred_element_type=jnp.float32,
    )
    fresh = lax.psum_scatter(partial_kv.astype(jnp.bfloat16), "tp", scatter_dimension=1, tiled=True)
    wanted = retrieval[0]
    blocks_dev = cache_table.shape[0]
    npool = lax.axis_size("pool")
    owners = wanted // blocks_dev
    local = wanted % blocks_dev
    hits = (owners[:, None] == jnp.arange(npool, dtype=jnp.int32)[None, :]).astype(jnp.int32)
    request = jnp.sum(hits * (local + 1)[:, None], axis=0)
    incoming = lax.all_to_all(
        request.reshape(npool, 1), "pool", split_axis=0, concat_axis=0, tiled=True
    ).reshape(npool)
    reply = jnp.zeros((npool,) + cache_table.shape[1:], jnp.bfloat16)
    for slot in range(blocks_dev):
        reply = jnp.where((incoming == slot + 1)[:, None, None], cache_table[slot][None], reply)
    arrived = lax.all_to_all(reply, "pool", split_axis=0, concat_axis=0, tiled=True)
    fetched = jnp.take(arrived, owners, axis=0)
    count = hidden_rows.shape[0]
    fetch_count = wanted.shape[0]
    group = QH // KVH
    scale = float(HD) ** (-0.5)
    local_heads = fresh.shape[1] // (2 * HD)
    width = fetched.shape[2]
    per_step = math.gcd(fetch_count, 8)
    steps_count = fetch_count // per_step
    grouped = fetched.reshape(steps_count, per_step * BLK, width)
    pat_steps = jnp.transpose(
        pattern[0].reshape(pattern.shape[1], steps_count, per_step), (1, 0, 2)
    )
    token_of_row = jnp.arange(count * group) // group
    block_of_row = token_of_row // RBLK
    row_blocks = block_of_row[:, None, None] == jnp.arange(pattern.shape[1])[None, :, None]
    near_mask = token_of_row[:, None] >= jnp.arange(count)[None, :]
    q_heads = queries.reshape(count, local_heads, group * HD)
    q_rows = q_heads[:, 0].reshape(count * group, HD)
    near_keys = fresh[:, 0:HD]
    near_vals = fresh[:, HD : 2 * HD]
    near_scores = rows_by_keys(q_rows, near_keys) * scale
    top = jnp.max(jnp.where(near_mask, near_scores, -1e30), axis=1)
    weights = jnp.where(near_mask, jnp.exp(near_scores - top[:, None]), 0.0)
    total = jnp.sum(weights, axis=1)
    numer = jnp.dot(weights.astype(jnp.bfloat16), near_vals, preferred_element_type=jnp.float32)

    def visit(carry, items):
        top_now, total_now, numer_now = carry
        block_rows, pat_now = items
        keys = block_rows[:, 0:HD]
        vals = block_rows[:, HD : 2 * HD]
        scores = rows_by_keys(q_rows, keys) * scale
        row_pat = jnp.any(row_blocks & (pat_now[None] != 0), axis=1)
        mask = jnp.repeat(row_pat, BLK, axis=1)
        top_new = jnp.maximum(top_now, jnp.max(jnp.where(mask, scores, -1e30), axis=1))
        weights_now = jnp.where(mask, jnp.exp(scores - top_new[:, None]), 0.0)
        factor = jnp.exp(top_now - top_new)
        total_new = total_now * factor + jnp.sum(weights_now, axis=1)
        numer_new = numer_now * factor[:, None] + jnp.dot(
            weights_now.astype(jnp.bfloat16), vals, preferred_element_type=jnp.float32
        )
        return ((top_new, total_new, numer_new), None)

    (top, total, numer), unused = lax.scan(visit, (top, total, numer), (grouped, pat_steps))
    results = (numer / total[:, None]).reshape(count, group * HD)
    attended = results.astype(jnp.bfloat16)
    return (attended, fresh)


def solution(mesh):
    placed = (
        P("pool", "tp"),
        P("tp", "pool"),
        P("pool", "tp"),
        P("pool", None, "tp"),
        P("pool", None),
        P("pool", None, None),
    )
    return jax.shard_map(
        body,
        mesh=mesh,
        in_specs=placed,
        out_specs=(P("pool", "tp"), P("pool", "tp")),
        check_vma=False,
    )
```

profile of v0, /device:TPU:24, one launch (start us, length us, event | category | flops | bytes accessed | tf_op | source)
XLA Modules:
  0.0 508.4 jit_solution(17769728993314333137)
XLA Ops:
  7.2 0.7 and_select_fusion.2
  7.9 0.1 select_reduce_fusion.1
  8.0 0.7 copy.22
  8.8 19.8 %all-to-all-start = ((s32[128,1,1]{2,1,0:T(1,128)}), s32[128,1,1]{2,1,0:T(1,128)S(1)}, u32[]{:S(2)}, u32[]{:S(2)}) async-start(s32[128,1,1]{2,1,0:T(1,128)} %copy.22), calls=%async_computation.1 | async-start | bytes 131072 | tf_op jit(solution)/shard_map/all_to_all | solution.py:34
  28.5 1.1 slice_bitcast_fusion.7
  29.6 14.4 %all-to-all-done = s32[128,1,1]{2,1,0:T(1,128)S(1)} async-done(((s32[128,1,1]{2,1,0:T(1,128)}), s32[128,1,1]{2,1,0:T(1,128)S(1)}, u32[]{:S(2)}, u32[]{:S(2)}) %all-to-all-start) | async-done | bytes 544 | tf_op jit(solution)/shard_map/all_to_all | solution.py:34
  44.0 18.3 %compare_reduce_fusion.7 = (pred[128]{0:T(512)(128)(4,1)S(1)}, pred[128]{0:T(512)(128)(4,1)S(1)}, pred[128]{0:T(512)(128)(4,1)S(1)}, pred[128]{0:T(512)(128)(4,1...) fusion(s32[128,1,1]{2,1,0:T(1,128)S(1)} %all-to-all-done), kind=kLoop, calls=%fused_computation.42 | loop fusion | flops 1024 | bytes 1536 | tf_op jit(solution)/shard_map/eq | solution.py:39
  62.4 7.7 %select_select_fusion = bf16[128,128,256]{2,1,0:T(8,128)(2,1)} fusion(pred[128]{0:T(512)(128)(4,1)S(1)} %get-tuple-element.107, pred[128]{0:T(512)(128)(4,1)S(1)} %get-tuple-element.108, pred[128]{0:T(512)(128)(4,1)S(1)} %get-tuple-element.109, pred[128]{0:T(512)(128)(4,1)S(1)} %get-tuple-element.110, pred[128]{0:T(512)(128)(4,1)S(1)} %get-tuple-element.111, ...), kind=kLoop, calls=%fused_computation.20 | loop fusion | flops 33554432 | bytes 8913920 | tf_op jit(solution)/shard_map/jit(_where)/select_n | solution.py:39
  70.1 7.6 %all-to-all-start.1 = ((bf16[128,128,256]{2,1,0:T(8,128)(2,1)}), bf16[128,128,256]{2,1,0:T(8,128)(2,1)}, u32[]{:S(2)}, u32[]{:S(2)}) async-start(bf16[128,128,256]{2,1,0:T(8,128)(2,1)} %select_select_fusion), calls=%async_computation.2 | async-start | bytes 16777216 | tf_op jit(solution)/shard_map/all_to_all | solution.py:40
  77.7 0.7 all-gather.2.cloned.1.call-update
  78.5 0.5 broadcast.347
  79.0 0.7 reduce.19
  79.7 0.1 squeeze.13
  79.8 0.1 copy.21
  79.9 0.1 reshape_squeeze_reshape.3
  80.1 198.2 %all-gather.2.cloned.1.call-done = bf16[2048,1024]{0,1:T(8,128)(2,1)} async-done(((bf16[2048,8]{0,1:T(8,128)(2,1)}), bf16[2048,1024]{0,1:T(8,128)(2,1)}) %all-gather.2.cloned.1.call-update) | async-done | bytes 4194320 | tf_op jit(solution)/shard_map/all_gather | solution.py:23
  278.3 4.4 convolution_convert_fusion
  282.8 28.2 %reduce-scatter.2.cloned.1.call-done = bf16[128,256]{1,0:T(8,128)(2,1)} async-done(((bf16[128,1024]{1,0:T(8,128)(2,1)}), bf16[128,256]{1,0:T(8,128)(2,1)}) %reduce-scatter.2.cloned.1.call-update) | async-done | bytes 65552 | tf_op jit(solution)/shard_map/reduce_scatter | solution.py:26
  311.1 1.0 select_reduce_fusion
  312.1 0.1 fusion.11
  312.2 1.0 fusion.12
  313.2 144.4 %all-to-all-done.1 = bf16[128,128,256]{2,1,0:T(8,128)(2,1)} async-done(((bf16[128,128,256]{2,1,0:T(8,128)(2,1)}), bf16[128,128,256]{2,1,0:T(8,128)(2,1)}, u32[]{:S(2)}, u32[]{:S(2)}) %all-to-all-start.1) | async-done | bytes 8388640 | tf_op jit(solution)/shard_map/all_to_all | solution.py:40
  457.7 6.2 %gather_fusion = bf16[64,128,256]{2,1,0:T(8,128)(2,1)} fusion(bf16[128,128,256]{2,1,0:T(8,128)(2,1)} %all-to-all-done.1, s32[1024]{0:T(1024)S(1)} %pad_clamp_fusion), kind=kCustom, calls=%fused_computation | custom fusion | bytes 8388864 | tf_op jit(solution)/shard_map/jit(_take)/gather | solution.py:41
  463.8 5.3 %bitcast_select_fusion.2 = bf16[8,1024,256]{2,1,0:T(8,128)(2,1)} fusion(pred[8,1024]{1,0:T(8,128)(4,1)S(1)} %broadcast_bitcast_fusion, bf16[8,1024,256]{2,1,0:T(8,128)(2,1)} %bitcast.104), kind=kLoop, calls=%fused_computation.21 | loop fusion | flops 2097152 | bytes 8396800 | tf_op jit(solution)/shard_map/jit(_take)/select_n | solution.py:41
  469.1 31.4 %while.15 = (s32[]{:T(128)}, f32[1024]{0:T(1024)S(1)}, f32[1024]{0:T(1024)S(1)}, f32[1024,128]{1,0:T(8,128)S(1)}, s32[8,2,8]{2,0,1:T(8,128)S(1)}, /*index=5*/bf1...) while((s32[]{:T(128)}, f32[1024]{0:T(1024)S(1)}, ...), condition=%wide.region_8.9_spmd.clone, body=%wide.region_4.8_spmd.clone.sunk | while | flops 545550336 | bytes 15561029 | solution.py:85
  469.2 0.1 and_reduce_fusion.2
  469.2 1.1 dynamic-slice_bitcast_fusion.2
  470.3 0.7 fusion.42
  471.1 0.9 fusion.43
  472.0 1.0 convolution_add_fusion.2
  473.2 1.1 dynamic-slice_bitcast_fusion.2
  474.2 0.7 fusion.42
  475.0 0.9 fusion.43
  476.0 1.0 convolution_add_fusion.2
  477.1 1.1 dynamic-slice_bitcast_fusion.2
  478.2 0.7 fusion.42
  478.9 0.9 fusion.43
  479.9 1.0 convolution_add_fusion.2
  480.9 0.1 and_reduce_fusion.2
  481.0 1.1 dynamic-slice_bitcast_fusion.2
  482.1 0.7 fusion.42
  482.9 0.9 fusion.43
  483.8 1.0 convolution_add_fusion.2
  484.9 0.1 and_reduce_fusion.2
  485.0 1.1 dynamic-slice_bitcast_fusion.2
  486.0 0.7 fusion.42
  486.8 0.9 fusion.43
  487.7 1.0 convolution_add_fusion.2
  488.8 0.1 and_reduce_fusion.2
  488.9 1.1 dynamic-slice_bitcast_fusion.2
  490.0 0.7 fusion.42
  490.7 0.9 fusion.43
  491.7 1.0 convolution_add_fusion.2
  492.8 1.1 dynamic-slice_bitcast_fusion.2
  493.9 0.7 fusion.42
  494.7 0.9 fusion.43
  495.6 1.0 convolution_add_fusion.2
  496.7 0.1 and_reduce_fusion.2
  496.7 1.1 dynamic-slice_bitcast_fusion.2
  497.8 0.7 fusion.42
  498.6 0.9 fusion.43
  499.5 1.0 convolution_add_fusion.2
  500.5 0.2 divide_convert_fusion
  500.8 0.8 convert_element_type.19
  (69 shorter events, 0.9 us)
Async XLA Ops:
  7.2 271.1 %copy-start = (bf16[128,2048]{1,0:T(8,128)(2,1)S(1)}, bf16[128,2048]{1,0:T(8,128)(2,1)}, u32[]{:S(2)}) copy-start(bf16[128,2048]{1,0:T(8,128)(2,1)} %param.8) | copy-start | bytes 1572868
  8.8 35.3 %all-to-all-start = ((s32[128,1,1]{2,1,0:T(1,128)}), s32[128,1,1]{2,1,0:T(1,128)S(1)}, u32[]{:S(2)}, u32[]{:S(2)}) async-start(s32[128,1,1]{2,1,0:T(1,128)} %copy.22), calls=%async_computation.1 | async-start | bytes 131072 | tf_op jit(solution)/shard_map/all_to_all | solution.py:34
  70.1 8.9 %copy-start.3 = (s32[1,64]{1,0:T(1,128)S(1)}, s32[1,64]{1,0:T(1,128)}, u32[]{:S(2)}) copy-start(s32[1,64]{1,0:T(1,128)} %param.12) | copy-start | bytes 772
  70.1 9.8 %copy-start.1 = (bf16[128,1024]{1,0:T(8,128)(2,1)S(1)}, bf16[128,1024]{1,0:T(8,128)(2,1)}, u32[]{:S(2)}) copy-start(bf16[128,1024]{1,0:T(8,128)(2,1)} %param.10) | copy-start | bytes 786436
  70.1 9.9 %copy-start.2 = (s32[1,2,64]{2,1,0:T(2,128)S(1)}, s32[1,2,64]{2,1,0:T(2,128)}, u32[]{:S(2)}) copy-start(s32[1,2,64]{2,1,0:T(2,128)} %param.13) | copy-start | bytes 1540
  70.1 387.6 %all-to-all-start.1 = ((bf16[128,128,256]{2,1,0:T(8,128)(2,1)}), bf16[128,128,256]{2,1,0:T(8,128)(2,1)}, u32[]{:S(2)}, u32[]{:S(2)}) async-start(bf16[128,128,256]{2,1,0:T(8,128)(2,1)} %select_select_fusion), calls=%async_computation.2 | async-start | bytes 16777216 | tf_op jit(solution)/shard_map/all_to_all | solution.py:40
  77.7 200.6 %all-gather.2.cloned.1.call-start = ((), (), s32[]{:S(2)}) async-start(), calls=%async_computation.3 | async-start | bytes 4227072 | tf_op jit(solution)/shard_map/all_gather | solution.py:23
  78.4 232.6 %reduce-scatter.2.cloned.1.call-start = ((), (), s32[]{:S(2)}) async-start(), calls=%async_computation.4 | async-start | bytes 327680 | tf_op jit(solution)/shard_map/reduce_scatter | solution.py:26
Sparse Core Ops, SparseCore 0:
  81.7 196.5 all-gather.1
  282.9 28.1 reduce-scatter.1
where the time goes:
time: 509 us; the launch traced here: 508 us
  waiting for transfers between devices  386 us (76%)
  other arithmetic  41.6 us (8%)
  starting transfers between devices  27.5 us (5%)
  matrix products  20.2 us (4%)
  local copies, waits for them, and re-layouts  18.5 us (4%)
  between operations  14.1 us (3%)
    all_gather x1, waiting for transfers between devices, body(): lax.all_gather(kv_weight, 'pool', axis=1, tiled=True)  198 us
    all_to_all x1, waiting for transfers between devices, body(): lax.all_to_all(reply, 'pool', split_axis=0, concat_axis=0, tiled=True)  144 us
    reduce_scatter x1, waiting for transfers between devices, body(): lax.psum_scatter(partial_kv.astype(jnp.bfloat16), 'tp', scatter_dimension...  28.2 us
    all_to_all x1, starting transfers between devices, body(): lax.all_to_all(request.reshape(npool, 1), 'pool', split_axis=0, concat_ax...  19.8 us
    eq x1, other arithmetic, body(): incoming == slot + 1  18.3 us
    all_to_all x1, waiting for transfers between devices, body(): lax.all_to_all(request.reshape(npool, 1), 'pool', split_axis=0, concat_ax...  14.4 us
  transfers between devices with their start and end apart: 4, of which 4 were waited for; matrix products, arithmetic and copies ran while one was open for 2% of the time, Pallas kernels for 0%

commit v1 on v0

--- a/solution.py
+++ b/solution.py
@@ -18,10 +18,14 @@
 
 
 def body(hidden_rows, kv_weight, queries, cache_table, retrieval, pattern):
+
+    def edit_grid_now(values, axis_no, axis_key):
+        v1 = jnp.stack([values for _ in range(lax.axis_size(axis_key))])
+        h_now = lax.all_to_all(v1, axis_name=axis_key, split_axis=0, concat_axis=0)
+        return jnp.concatenate(h_now, axis_no)
+
     partial_kv = jnp.dot(
-        hidden_rows,
-        lax.all_gather(kv_weight, "pool", axis=1, tiled=True),
-        preferred_element_type=jnp.float32,
+        hidden_rows, edit_grid_now(kv_weight, 1, "pool"), preferred_element_type=jnp.float32
     )
     fresh = lax.psum_scatter(partial_kv.astype(jnp.bfloat16), "tp", scatter_dimension=1, tiled=True)
     wanted = retrieval[0]

time: 509 us -> 670 us (1.32)
  waiting for transfers between devices: 386 us -> 519 us
  blocking collectives: 0 us -> 35.1 us
  starting transfers between devices: 27.5 us -> 18.6 us
    all_gather x1 -> x0, waiting for transfers between devices: 198 us -> none  [body(): lax.all_gather(kv_weight, 'pool', axis=1, tiled=True)]
    all_to_all x1, waiting for transfers between devices: 144 us -> 331 us  [body(): lax.all_to_all(reply, 'pool', split_axis=0, concat_axis=0, tiled=True)]
    all_to_all x1, waiting for transfers between devices: 14.4 us -> 161 us  [edit_grid_now(): h_now = lax.all_to_all(v1, axis_name=axis_key, split_axis=0, concat_axis=0)]
    all_to_all x0 -> x1, blocking collectives: none -> 35.1 us  [body(): lax.all_to_all(request.reshape(npool, 1), 'pool', split_axis=0, concat_ax...]
    all_to_all x1, starting transfers between devices: 19.8 us -> 7.69 us  [edit_grid_now(): h_now = lax.all_to_all(v1, axis_name=axis_key, split_axis=0, concat_axis=0)]
  transfers between devices with their start and end apart: 4 -> 3, of which waited for: 4 -> 3; matrix products, arithmetic and copies ran while one was open for 2% -> 5% of each run, Pallas kernels for 0% -> 0%
where the time goes in v1:
time: 670 us; the launch traced here: 669 us
  waiting for transfers between devices  519 us (77%)
  other arithmetic  41.7 us (6%)
  blocking collectives  35.1 us (5%)
  matrix products  20.2 us (3%)
  local copies, waits for them, and re-layouts  20 us (3%)
  starting transfers between devices  18.6 us (3%)
  between operations  14.2 us (2%)
    all_to_all x1, waiting for transfers between devices, body(): lax.all_to_all(reply, 'pool', split_axis=0, concat_axis=0, tiled=True)  331 us
    all_to_all x1, waiting for transfers between devices, edit_grid_now(): h_now = lax.all_to_all(v1, axis_name=axis_key, split_axis=0, concat_axis=0)  161 us
    all_to_all x1, blocking collectives, body(): lax.all_to_all(request.reshape(npool, 1), 'pool', split_axis=0, concat_ax...  35.1 us
    reduce_scatter x1, waiting for transfers between devices, body(): lax.psum_scatter(partial_kv.astype(jnp.bfloat16), 'tp', scatter_dimension...  27.6 us
    eq x1, other arithmetic, body(): incoming == slot + 1  18.4 us
  transfers between devices with their start and end apart: 3, of which 3 were waited for; matrix products, arithmetic and copies ran while one was open for 5% of the time, Pallas kernels for 0%

profile of v1, /device:TPU:24, one launch (start us, length us, event | category | flops | bytes accessed | tf_op | source)
XLA Modules:
  0.0 669.4 jit_solution(5710430382484247807)
XLA Ops:
  7.2 0.7 and_select_fusion.2
  7.9 0.1 select_reduce_fusion.1
  8.0 0.1 copy.23
  8.1 35.1 %all_to_all.19 = s32[128,1,1]{2,1,0:T(1,128)S(1)} all-to-all(s32[128,1,1]{2,1,0:T(1,128)S(1)} %copy.23), channel_id=1, replica_groups=mesh['pool'=128,'tp'=4] {'pool'}, dimensions={0} | all-to-all | bytes 1024 | tf_op jit(solution)/shard_map/all_to_all | solution.py:38
  43.2 3.2 stack.2
  46.4 7.7 %all-to-all-start = ((bf16[128,2048,8]{1,2,0:T(8,128)(2,1)}), bf16[128,2048,8]{1,2,0:T(8,128)(2,1)}, u32[]{:S(2)}, u32[]{:S(2)}) async-start(bf16[128,2048,8]{1,2,0:T(8,128)(2,1)} %stack.2), calls=%async_computation | async-start | bytes 8388608 | tf_op jit(solution)/shard_map/all_to_all | solution.py:24
  54.2 18.4 %compare_reduce_fusion.7 = (pred[128]{0:T(512)(128)(4,1)S(1)}, pred[128]{0:T(512)(128)(4,1)S(1)}, pred[128]{0:T(512)(128)(4,1)S(1)}, pred[128]{0:T(512)(128)(4,1...) fusion(s32[128,1,1]{2,1,0:T(1,128)S(1)} %all_to_all.19), kind=kLoop, calls=%fused_computation.44 | loop fusion | flops 1024 | bytes 1536 | tf_op jit(solution)/shard_map/eq | solution.py:43
  72.6 7.8 %select_select_fusion = bf16[128,128,256]{2,1,0:T(8,128)(2,1)} fusion(pred[128]{0:T(512)(128)(4,1)S(1)} %get-tuple-element.107, pred[128]{0:T(512)(128)(4,1)S(1)} %get-tuple-element.108, pred[128]{0:T(512)(128)(4,1)S(1)} %get-tuple-element.109, pred[128]{0:T(512)(128)(4,1)S(1)} %get-tuple-element.110, pred[128]{0:T(512)(128)(4,1)S(1)} %get-tuple-element.111, ...), kind=kLoop, calls=%fused_computation.20 | loop fusion | flops 33554432 | bytes 8913920 | tf_op jit(solution)/shard_map/jit(_where)/select_n | solution.py:43
  80.4 160.6 %all-to-all-done = bf16[128,2048,8]{1,2,0:T(8,128)(2,1)} async-done(((bf16[128,2048,8]{1,2,0:T(8,128)(2,1)}), bf16[128,2048,8]{1,2,0:T(8,128)(2,1)}, u32[]{:S(2)}, u32[]{:S(2)}) %all-to-all-start) | async-done | bytes 4194336 | tf_op jit(solution)/shard_map/all_to_all | solution.py:24
  241.0 10.8 %all-to-all-start.2 = ((bf16[128,128,256]{2,1,0:T(8,128)(2,1)}), bf16[128,128,256]{2,1,0:T(8,128)(2,1)}, u32[]{:S(2)}, u32[]{:S(2)}) async-start(bf16[128,128,256]{2,1,0:T(8,128)(2,1)} %select_select_fusion), calls=%async_computation.3 | async-start | bytes 16777216 | tf_op jit(solution)/shard_map/all_to_all | solution.py:44
  251.9 0.5 broadcast.349
  252.4 0.7 reduce.19
  253.1 0.1 squeeze.13
  253.2 0.1 copy.22
  253.2 0.1 reshape_squeeze_reshape.3
  253.5 4.4 fusion.12
  258.0 27.6 %reduce-scatter.2.cloned.1.call-done = bf16[128,256]{1,0:T(8,128)(2,1)} async-done(((bf16[128,1024]{1,0:T(8,128)(2,1)}), bf16[128,256]{1,0:T(8,128)(2,1)}) %reduce-scatter.2.cloned.1.call-update) | async-done | bytes 65552 | tf_op jit(solution)/shard_map/reduce_scatter | solution.py:30
  285.7 1.0 select_reduce_fusion
  286.7 0.1 fusion.16
  286.8 1.0 fusion.17
  287.9 330.8 %all-to-all-done.2 = bf16[128,128,256]{2,1,0:T(8,128)(2,1)} async-done(((bf16[128,128,256]{2,1,0:T(8,128)(2,1)}), bf16[128,128,256]{2,1,0:T(8,128)(2,1)}, u32[]{:S(2)}, u32[]{:S(2)}) %all-to-all-start.2) | async-done | bytes 8388640 | tf_op jit(solution)/shard_map/all_to_all | solution.py:44
  618.6 6.2 gather_fusion
  624.8 5.3 bitcast_select_fusion.2
  630.1 31.4 %while.15 = (s32[]{:T(128)}, f32[1024]{0:T(1024)S(1)}, f32[1024]{0:T(1024)S(1)}, f32[1024,128]{1,0:T(8,128)S(1)}, s32[8,2,8]{2,0,1:T(8,128)S(1)}, /*index=5*/bf1...) while((s32[]{:T(128)}, f32[1024]{0:T(1024)S(1)}, ...), condition=%wide.region_8.9_spmd.clone, body=%wide.region_4.8_spmd.clone.sunk | while | flops 545550336 | bytes 15561029 | solution.py:89
  630.1 0.1 and_reduce_fusion.2
  630.2 1.1 dynamic-slice_bitcast_fusion.2
  631.3 0.7 fusion.46
  632.0 0.9 fusion.47
  633.0 1.0 convolution_add_fusion.2
  634.0 0.1 and_reduce_fusion.2
  634.1 1.1 dynamic-slice_bitcast_fusion.2
  635.2 0.7 fusion.46
  636.0 0.9 fusion.47
  636.9 1.0 convolution_add_fusion.2
  638.1 1.1 dynamic-slice_bitcast_fusion.2
  639.1 0.7 fusion.46
  639.9 0.9 fusion.47
  640.8 1.0 convolution_add_fusion.2
  641.9 0.1 and_reduce_fusion.2
  642.0 1.1 dynamic-slice_bitcast_fusion.2
  643.1 0.7 fusion.46
  643.8 0.9 fusion.47
  644.8 1.0 convolution_add_fusion.2
  645.8 0.1 and_reduce_fusion.2
  645.9 1.1 dynamic-slice_bitcast_fusion.2
  647.0 0.7 fusion.46
  647.8 0.9 fusion.47
  648.7 1.0 convolution_add_fusion.2
  649.8 0.1 and_reduce_fusion.2
  649.8 1.1 dynamic-slice_bitcast_fusion.2
  650.9 0.7 fusion.46
  651.7 0.9 fusion.47
  652.6 1.0 convolution_add_fusion.2
  653.8 1.1 dynamic-slice_bitcast_fusion.2
  654.9 0.7 fusion.46
  655.6 0.9 fusion.47
  656.6 1.0 convolution_add_fusion.2
  657.6 0.1 and_reduce_fusion.2
  657.7 1.1 dynamic-slice_bitcast_fusion.2
  658.8 0.7 fusion.46
  659.5 0.9 fusion.47
  660.5 1.0 convolution_add_fusion.2
  661.5 0.2 divide_convert_fusion
  661.7 0.8 convert_element_type.19
  (70 shorter events, 0.8 us)
Async XLA Ops:
  7.2 246.3 %copy-start = (bf16[128,2048]{1,0:T(8,128)(2,1)S(1)}, bf16[128,2048]{1,0:T(8,128)(2,1)}, u32[]{:S(2)}) copy-start(bf16[128,2048]{1,0:T(8,128)(2,1)} %param.8) | copy-start | bytes 1572868
  46.4 7.7 %copy-start.1 = (bf16[8,128,256]{2,1,0:T(8,128)(2,1)S(1)}, bf16[8,128,256]{2,1,0:T(8,128)(2,1)}, u32[]{:S(2)}) copy-start(bf16[8,128,256]{2,1,0:T(8,128)(2,1)} %param.11) | copy-start | bytes 1572868
  46.4 194.5 %all-to-all-start = ((bf16[128,2048,8]{1,2,0:T(8,128)(2,1)}), bf16[128,2048,8]{1,2,0:T(8,128)(2,1)}, u32[]{:S(2)}, u32[]{:S(2)}) async-start(bf16[128,2048,8]{1,2,0:T(8,128)(2,1)} %stack.2), calls=%async_computation | async-start | bytes 8388608 | tf_op jit(solution)/shard_map/all_to_all | solution.py:24
  80.4 172.0 %copy-start.4 = (s32[1,64]{1,0:T(1,128)S(1)}, s32[1,64]{1,0:T(1,128)}, u32[]{:S(2)}) copy-start(s32[1,64]{1,0:T(1,128)} %param.12) | copy-start | bytes 772
  80.4 172.9 %copy-start.2 = (bf16[128,1024]{1,0:T(8,128)(2,1)S(1)}, bf16[128,1024]{1,0:T(8,128)(2,1)}, u32[]{:S(2)}) copy-start(bf16[128,1024]{1,0:T(8,128)(2,1)} %param.10) | copy-start | bytes 786436
  80.4 173.0 %copy-start.3 = (s32[1,2,64]{2,1,0:T(2,128)S(1)}, s32[1,2,64]{2,1,0:T(2,128)}, u32[]{:S(2)}) copy-start(s32[1,2,64]{2,1,0:T(2,128)} %param.13) | copy-start | bytes 1540
  241.0 377.7 %all-to-all-start.2 = ((bf16[128,128,256]{2,1,0:T(8,128)(2,1)}), bf16[128,128,256]{2,1,0:T(8,128)(2,1)}, u32[]{:S(2)}, u32[]{:S(2)}) async-start(bf16[128,128,256]{2,1,0:T(8,128)(2,1)} %select_select_fusion), calls=%async_computation.3 | async-start | bytes 16777216 | tf_op jit(solution)/shard_map/all_to_all | solution.py:44
  251.8 33.8 %reduce-scatter.2.cloned.1.call-start = ((), (), s32[]{:S(2)}) async-start(), calls=%async_computation.4 | async-start | bytes 327680 | tf_op jit(solution)/shard_map/reduce_scatter | solution.py:30
Sparse Core Ops, SparseCore 0:
  258.0 27.5 reduce-scatter.1
